TPU v7x, 128 devices: a whole 4x4x4 slice. The times are simulated.
128 devices in a mesh: depth: 8 (over z, core), plane: 16 (over x, y).
Axes of the slice: x: 4, y: 4, z: 4, core: 2. Of those that a mesh axis runs over, the one named last changes fastest.
Arguments:
- toar: bfloat16 [8, 8, 2, 32768], P('depth', None, None, 'plane'), may hold values from -6 to 6
- pml_coeff: float32 [8, 2, 32768], P('depth', None, 'plane'), may hold values from -1.5 to 1.5
- coupling: float32 [8, 32768], P('depth', 'plane'), may hold values from 0.5 to 1
- inverse: bfloat16 [8, 512, 16, 64, 128], P('depth', 'plane'), may hold values from -0.125 to 0.125
- pattern: int32 [8, 512, 16], P('depth', 'plane'), may hold values from 0 to 511
- patch_map: int32 [8, 32768], P('depth', 'plane'), may hold values from 0 to 16383, as said below
Outputs:
- precond: bfloat16 [8, 8, 2, 32768], P('depth', None, None, 'plane')
- patch_sens: float32 [8, 16384], P(None, ('depth', 'plane'))
Inputs may be any that keep to these rules, and one draw needn't show every extreme that they name: `patch_map`: patch p belongs to owner p // 128. Among the cells of one device (one layer, one block of 2048 cells), at most 32 name patches of any one owner, and in every such block some owner is named exactly 32 times. `pattern`: block columns of the whole layer.
All inputs are finite; a program needn't handle non-finite values.
Results may differ from a plain program's by a relative error of at most 0.018.
Values may be sent and summed in bfloat16 or wider, within the bound.
No kernel may reach another device: no remote copies, remote signals or barrier semaphores. Data moves between devices by JAX's collectives and lax.ppermute only.
A program may use at most 128 MiB of HBM per device.

v0:
```python
import jax
import jax.numpy as jnp
from jax import lax
from jax.sharding import PartitionSpec as P

PATCH_DEV = 128


def passed_along(value, axis, steps):
    count = lax.axis_size(axis)
    first, last = (max(0, -steps), min(count, count - steps))
    return lax.ppermute(value, axis, [(source, source + steps) for source in range(first, last)])


def shards(toar, pml_coeff, coupling, inverse, pattern, patch_map):
    toar_local = toar[0]
    coeff = pml_coeff[0]
    coupler = coupling[0]
    inv_local = inverse[0]
    pattern_flat = pattern[0].reshape(-1)
    block_rows = inv_local.shape[0]
    per_row = inv_local.shape[1]
    block_cells = inv_local.shape[2]
    depth_count = lax.axis_size("depth")
    factor = inv_local.reshape(block_rows, per_row, block_cells, 2, block_cells)
    toar_f32 = toar_local.astype(jnp.float32)
    real_part = coeff[0] * toar_f32[:, 0] - coeff[1] * toar_f32[:, 1]
    imag_part = coeff[0] * toar_f32[:, 1] + coeff[1] * toar_f32[:, 0]
    source = jnp.stack([real_part, imag_part], axis=1)

    def apply_layer(incoming):
        gathered = lax.all_gather(incoming, "plane", axis=2, tiled=True)
        rows_here = gathered.shape[0]
        blocks = gathered.reshape(rows_here, 2, -1, block_cells)
        chosen = jnp.take(blocks, pattern_flat, axis=2)
        chosen = chosen.reshape(rows_here, 2, block_rows, per_row, block_cells)
        partial_value = jnp.einsum(
            "rkiaj,vbrkj->vabri", factor, chosen, preferred_element_type=jnp.float32
        )
        real_out = partial_value[:, 0, 0] - partial_value[:, 1, 1]
        imag_out = partial_value[:, 0, 1] + partial_value[:, 1, 0]
        return jnp.stack([real_out, imag_out], axis=1).reshape(
            rows_here, 2, block_rows * block_cells
        )

    def down_turn(turn_index, current):
        arrived = passed_along(current, "depth", 1)
        down_in = (source + coupler * arrived.astype(jnp.float32)).astype(jnp.bfloat16)
        return apply_layer(down_in).astype(jnp.bfloat16)

    first = apply_layer(source.astype(jnp.bfloat16)).astype(jnp.bfloat16)
    swept = lax.fori_loop(0, depth_count - 1, down_turn, first)

    def up_turn(turn_index, current):
        outgoing = (coupler * current.astype(jnp.float32)).astype(jnp.bfloat16)
        arrived = passed_along(outgoing, "depth", -1)
        return (swept.astype(jnp.float32) + apply_layer(arrived)).astype(jnp.bfloat16)

    precond = lax.fori_loop(0, depth_count - 1, up_turn, swept)
    product = precond.astype(jnp.float32) * toar_f32
    contrib = product[:, 0] + product[:, 1]
    cell_patch = patch_map[0]
    owner_count = depth_count * lax.axis_size("plane")
    patch_total = PATCH_DEV * owner_count
    local_sums = jax.ops.segment_sum(contrib.T, cell_patch, num_segments=patch_total).T
    owned = lax.psum_scatter(local_sums, ("depth", "plane"), scatter_dimension=1, tiled=True)
    return (precond[None], owned)


def solution(mesh):
    return jax.shard_map(
        shards,
        mesh=mesh,
        in_specs=(
            P("depth", None, None, "plane"),
            P("depth", None, "plane"),
            P("depth", "plane"),
            P("depth", "plane", None, None, None),
            P("depth", "plane", None),
            P("depth", "plane"),
        ),
        out_specs=(P("depth", None, None, "plane"), P(None, ("depth", "plane"))),
        check_vma=False,
    )
```

profile of v0, /device:TPU:0, one launch (start us, length us, event | category | flops | bytes accessed | tf_op | source)
XLA Modules:
  0.0 1754.3 jit_solution(11908913365908243737)
XLA Ops:
  10.4 27.9 %reshape_squeeze.7 = bf16[32,16,64,2,64]{4,3,2,1,0:T(2,128)(2,1)} reshape(bf16[1,32,16,64,128]{4,3,2,1,0:T(8,128)(2,1)} %param.15) | data formatting | bytes 16777216 | tf_op jit(solution)/shard_map/reshape;squeeze | solution.py:25
  38.3 15.2 copy.28
  67.1 13.0 fusion.24
  80.5 501.8 %while.20 = (s32[]{:T(128)}, bf16[8,2,2048]{2,0,1:T(8,128)(2,1)S(1)}, f32[1,2048]{1,0:T(1,128)S(1)}, f32[8,2,2048]{2,0,1:T(8,128)S(1)}, s32[512]{0:T(512)S(1)}, /*index=5*/bf16[32,16,64,2,64]{4,2,1,3,0:T(8,128)(2,1)}, s32[]{:T(128)}) while((s32[]{:T(128)}, bf16[8,2,2048]{2,0,1:T(8,128)(2,1)S(1)}, f32[1,2048]{1,0:T(1,128)S(1)}, ...), condition=%wide.region_1.3_spmd, body=%wide.region_0.0_spmd.sunk | while | flops 134977024 | bytes 22699164 | solution.py:52
  83.6 46.3 %all-gather.6.cloned.1.call-done = bf16[8,2,32768]{2,0,1:T(8,128)(2,1)} async-done(((bf16[8,2,2048]{2,0,1:T(8,128)(2,1)}), bf16[8,2,32768]{2,0,1:T(8,128)(2,1)}) %all-gather.6.cloned.1.call-update) | async-done | bytes 1048592 | tf_op jit(solution)/shard_map/while/body/eval_jaxpr/all_gather | solution.py:32
  135.6 4.1 gather_fusion
  142.7 10.1 fusion.44
  156.1 45.4 %all-gather.6.cloned.1.call-done = bf16[8,2,32768]{2,0,1:T(8,128)(2,1)} async-done(((bf16[8,2,2048]{2,0,1:T(8,128)(2,1)}), bf16[8,2,32768]{2,0,1:T(8,128)(2,1)}) %all-gather.6.cloned.1.call-update) | async-done | bytes 1048592 | tf_op jit(solution)/shard_map/while/body/eval_jaxpr/all_gather | solution.py:32
  207.2 4.1 gather_fusion
  214.2 10.1 fusion.44
  227.6 45.4 %all-gather.6.cloned.1.call-done = bf16[8,2,32768]{2,0,1:T(8,128)(2,1)} async-done(((bf16[8,2,2048]{2,0,1:T(8,128)(2,1)}), bf16[8,2,32768]{2,0,1:T(8,128)(2,1)}) %all-gather.6.cloned.1.call-update) | async-done | bytes 1048592 | tf_op jit(solution)/shard_map/while/body/eval_jaxpr/all_gather | solution.py:32
  278.7 4.1 gather_fusion
  285.7 10.1 fusion.44
  299.1 45.4 %all-gather.6.cloned.1.call-done = bf16[8,2,32768]{2,0,1:T(8,128)(2,1)} async-done(((bf16[8,2,2048]{2,0,1:T(8,128)(2,1)}), bf16[8,2,32768]{2,0,1:T(8,128)(2,1)}) %all-gather.6.cloned.1.call-update) | async-done | bytes 1048592 | tf_op jit(solution)/shard_map/while/body/eval_jaxpr/all_gather | solution.py:32
  350.2 4.1 gather_fusion
  357.3 10.1 fusion.44
  370.7 45.4 %all-gather.6.cloned.1.call-done = bf16[8,2,32768]{2,0,1:T(8,128)(2,1)} async-done(((bf16[8,2,2048]{2,0,1:T(8,128)(2,1)}), bf16[8,2,32768]{2,0,1:T(8,128)(2,1)}) %all-gather.6.cloned.1.call-update) | async-done | bytes 1048592 | tf_op jit(solution)/shard_map/while/body/eval_jaxpr/all_gather | solution.py:32
  421.8 4.1 gather_fusion
  428.8 10.1 fusion.44
  442.2 45.4 %all-gather.6.cloned.1.call-done = bf16[8,2,32768]{2,0,1:T(8,128)(2,1)} async-done(((bf16[8,2,2048]{2,0,1:T(8,128)(2,1)}), bf16[8,2,32768]{2,0,1:T(8,128)(2,1)}) %all-gather.6.cloned.1.call-update) | async-done | bytes 1048592 | tf_op jit(solution)/shard_map/while/body/eval_jaxpr/all_gather | solution.py:32
  493.3 4.1 gather_fusion
  500.3 10.1 fusion.44
  513.7 45.4 %all-gather.6.cloned.1.call-done = bf16[8,2,32768]{2,0,1:T(8,128)(2,1)} async-done(((bf16[8,2,2048]{2,0,1:T(8,128)(2,1)}), bf16[8,2,32768]{2,0,1:T(8,128)(2,1)}) %all-gather.6.cloned.1.call-update) | async-done | bytes 1048592 | tf_op jit(solution)/shard_map/while/body/eval_jaxpr/all_gather | solution.py:32
  571.8 10.1 fusion.44
  582.3 495.5 %while.21 = (s32[]{:T(128)}, bf16[8,2,2048]{2,0,1:T(8,128)(2,1)S(1)}, bf16[8,2,2048]{2,0,1:T(8,128)(2,1)S(1)}, f32[1,2048]{1,0:T(1,128)S(1)}, s32[512]{0:T(512)S...) while((s32[]{:T(128)}, bf16[8,2,2048]{2,0,1:T(8,128)(2,1)S(1)}, bf16[8,2,2048]{2,0,1:T(8,128)(2,1)S(1)}, ...), condition=%wide.region_3.5_spmd, body=%wide.region_2.4_spmd.sunk | while | flops 135009792 | bytes 23289016 | solution.py:59
  586.3 43.7 %all-gather.8.cloned.1.call-done = bf16[8,2,32768]{2,0,1:T(8,128)(2,1)} async-done(((bf16[8,2,2048]{2,0,1:T(8,128)(2,1)}), bf16[8,2,32768]{2,0,1:T(8,128)(2,1)}) %all-gather.8.cloned.1.call-update) | async-done | bytes 1048592 | tf_op jit(solution)/shard_map/while/body/eval_jaxpr/all_gather | solution.py:32
  635.7 4.1 gather_fusion.1
  642.7 10.1 fusion.48
  657.0 43.7 %all-gather.8.cloned.1.call-done = bf16[8,2,32768]{2,0,1:T(8,128)(2,1)} async-done(((bf16[8,2,2048]{2,0,1:T(8,128)(2,1)}), bf16[8,2,32768]{2,0,1:T(8,128)(2,1)}) %all-gather.8.cloned.1.call-update) | async-done | bytes 1048592 | tf_op jit(solution)/shard_map/while/body/eval_jaxpr/all_gather | solution.py:32
  706.4 4.1 gather_fusion.1
  713.5 10.1 fusion.48
  727.8 43.7 %all-gather.8.cloned.1.call-done = bf16[8,2,32768]{2,0,1:T(8,128)(2,1)} async-done(((bf16[8,2,2048]{2,0,1:T(8,128)(2,1)}), bf16[8,2,32768]{2,0,1:T(8,128)(2,1)}) %all-gather.8.cloned.1.call-update) | async-done | bytes 1048592 | tf_op jit(solution)/shard_map/while/body/eval_jaxpr/all_gather | solution.py:32
  777.2 4.1 gather_fusion.1
  784.3 10.1 fusion.48
  798.6 43.7 %all-gather.8.cloned.1.call-done = bf16[8,2,32768]{2,0,1:T(8,128)(2,1)} async-done(((bf16[8,2,2048]{2,0,1:T(8,128)(2,1)}), bf16[8,2,32768]{2,0,1:T(8,128)(2,1)}) %all-gather.8.cloned.1.call-update) | async-done | bytes 1048592 | tf_op jit(solution)/shard_map/while/body/eval_jaxpr/all_gather | solution.py:32
  848.0 4.1 gather_fusion.1
  855.0 10.1 fusion.48
  869.4 43.7 %all-gather.8.cloned.1.call-done = bf16[8,2,32768]{2,0,1:T(8,128)(2,1)} async-done(((bf16[8,2,2048]{2,0,1:T(8,128)(2,1)}), bf16[8,2,32768]{2,0,1:T(8,128)(2,1)}) %all-gather.8.cloned.1.call-update) | async-done | bytes 1048592 | tf_op jit(solution)/shard_map/while/body/eval_jaxpr/all_gather | solution.py:32
  918.8 4.1 gather_fusion.1
  925.8 10.1 fusion.48
  940.2 43.7 %all-gather.8.cloned.1.call-done = bf16[8,2,32768]{2,0,1:T(8,128)(2,1)} async-done(((bf16[8,2,2048]{2,0,1:T(8,128)(2,1)}), bf16[8,2,32768]{2,0,1:T(8,128)(2,1)}) %all-gather.8.cloned.1.call-update) | async-done | bytes 1048592 | tf_op jit(solution)/shard_map/while/body/eval_jaxpr/all_gather | solution.py:32
  989.6 4.1 gather_fusion.1
  996.6 10.1 fusion.48
  1010.9 43.7 %all-gather.8.cloned.1.call-done = bf16[8,2,32768]{2,0,1:T(8,128)(2,1)} async-done(((bf16[8,2,2048]{2,0,1:T(8,128)(2,1)}), bf16[8,2,32768]{2,0,1:T(8,128)(2,1)}) %all-gather.8.cloned.1.call-update) | async-done | bytes 1048592 | tf_op jit(solution)/shard_map/while/body/eval_jaxpr/all_gather | solution.py:32
  1060.3 4.1 gather_fusion.1
  1067.4 10.1 fusion.48
  1078.3 15.5 scatter_custom_fusion
  1094.5 651.7 %reduce-scatter.2.cloned.1.call-done = f32[8,128]{0,1:T(8,128)} async-done(((f32[8,16384]{0,1:T(8,128)}), f32[8,128]{0,1:T(8,128)}) %reduce-scatter.2.cloned.1.call-update) | async-done | bytes 4112 | tf_op jit(solution)/shard_map/reduce_scatter | solution.py:66
  (288 shorter events, 196.4 us)
Async XLA Ops:
  7.2 48.7 %all-gather.4.cloned.1.call-start = ((), (), s32[]{:S(2)}) async-start(), calls=%async_computation.1 | async-start | bytes 1114112 | tf_op jit(solution)/shard_map/all_gather | solution.py:32
  67.1 13.4 copy-start.1
  80.7 49.2 %all-gather.6.cloned.1.call-start = ((), (), s32[]{:S(2)}) async-start(), calls=%async_computation.3 | async-start | bytes 1114112 | tf_op jit(solution)/shard_map/while/body/eval_jaxpr/all_gather | solution.py:32
  80.7 2.2 collective-permute-start
  153.1 48.3 %all-gather.6.cloned.1.call-start = ((), (), s32[]{:S(2)}) async-start(), calls=%async_computation.3 | async-start | bytes 1114112 | tf_op jit(solution)/shard_map/while/body/eval_jaxpr/all_gather | solution.py:32
  153.2 2.2 collective-permute-start
  224.7 48.3 %all-gather.6.cloned.1.call-start = ((), (), s32[]{:S(2)}) async-start(), calls=%async_computation.3 | async-start | bytes 1114112 | tf_op jit(solution)/shard_map/while/body/eval_jaxpr/all_gather | solution.py:32
  224.7 2.2 collective-permute-start
  296.2 48.3 %all-gather.6.cloned.1.call-start = ((), (), s32[]{:S(2)}) async-start(), calls=%async_computation.3 | async-start | bytes 1114112 | tf_op jit(solution)/shard_map/while/body/eval_jaxpr/all_gather | solution.py:32
  296.2 2.2 collective-permute-start
  367.7 48.3 %all-gather.6.cloned.1.call-start = ((), (), s32[]{:S(2)}) async-start(), calls=%async_computation.3 | async-start | bytes 1114112 | tf_op jit(solution)/shard_map/while/body/eval_jaxpr/all_gather | solution.py:32
  367.8 2.2 collective-permute-start
  439.2 48.3 %all-gather.6.cloned.1.call-start = ((), (), s32[]{:S(2)}) async-start(), calls=%async_computation.3 | async-start | bytes 1114112 | tf_op jit(solution)/shard_map/while/body/eval_jaxpr/all_gather | solution.py:32
  439.3 2.2 collective-permute-start
  510.8 48.3 %all-gather.6.cloned.1.call-start = ((), (), s32[]{:S(2)}) async-start(), calls=%async_computation.3 | async-start | bytes 1114112 | tf_op jit(solution)/shard_map/while/body/eval_jaxpr/all_gather | solution.py:32
  510.8 2.2 collective-permute-start
  582.3 495.5 %copy-start.2 = (bf16[1,8,2,2048]{3,2,1,0:T(2,128)(2,1)S(1)}, bf16[1,8,2,2048]{3,2,1,0:T(2,128)(2,1)}, u32[]{:S(2)}) copy-start(bf16[1,8,2,2048]{3,2,1,0:T(2,128)(2,1)} %param.12) | copy-start | bytes 196612
  582.3 47.6 %all-gather.8.cloned.1.call-start = ((), (), s32[]{:S(2)}) async-start(), calls=%async_computation.4 | async-start | bytes 1114112 | tf_op jit(solution)/shard_map/while/body/eval_jaxpr/all_gather | solution.py:32
  582.4 3.1 collective-permute-start.1
  585.6 0.6 copy-start
  653.1 47.6 %all-gather.8.cloned.1.call-start = ((), (), s32[]{:S(2)}) async-start(), calls=%async_computation.4 | async-start | bytes 1114112 | tf_op jit(solution)/shard_map/while/body/eval_jaxpr/all_gather | solution.py:32
  653.2 3.1 collective-permute-start.1
  656.3 0.6 copy-start
  723.9 47.6 %all-gather.8.cloned.1.call-start = ((), (), s32[]{:S(2)}) async-start(), calls=%async_computation.4 | async-start | bytes 1114112 | tf_op jit(solution)/shard_map/while/body/eval_jaxpr/all_gather | solution.py:32
  724.0 3.1 collective-permute-start.1
  727.1 0.6 copy-start
  794.7 47.6 %all-gather.8.cloned.1.call-start = ((), (), s32[]{:S(2)}) async-start(), calls=%async_computation.4 | async-start | bytes 1114112 | tf_op jit(solution)/shard_map/while/body/eval_jaxpr/all_gather | solution.py:32
  794.8 3.1 collective-permute-start.1
  797.9 0.6 copy-start
  865.5 47.6 %all-gather.8.cloned.1.call-start = ((), (), s32[]{:S(2)}) async-start(), calls=%async_computation.4 | async-start | bytes 1114112 | tf_op jit(solution)/shard_map/while/body/eval_jaxpr/all_gather | solution.py:32
  865.5 3.1 collective-permute-start.1
  868.7 0.6 copy-start
  936.2 47.6 %all-gather.8.cloned.1.call-start = ((), (), s32[]{:S(2)}) async-start(), calls=%async_computation.4 | async-start | bytes 1114112 | tf_op jit(solution)/shard_map/while/body/eval_jaxpr/all_gather | solution.py:32
  936.3 3.1 collective-permute-start.1
  939.5 0.6 copy-start
  1007.0 47.6 %all-gather.8.cloned.1.call-start = ((), (), s32[]{:S(2)}) async-start(), calls=%async_computation.4 | async-start | bytes 1114112 | tf_op jit(solution)/shard_map/while/body/eval_jaxpr/all_gather | solution.py:32
  1007.1 3.1 collective-permute-start.1
  1010.2 0.6 copy-start
  1077.8 668.4 %reduce-scatter.2.cloned.1.call-start = ((), (), s32[]{:S(2)}) async-start(), calls=%async_computation.2 | async-start | bytes 8454144 | tf_op jit(solution)/shard_map/reduce_scatter | solution.py:66
Sparse Core Ops, SparseCore 0:
  10.8 45.0 all-gather.3
  84.6 45.3 all-gather.5
  157.0 44.4 all-gather.5
  228.2 44.7 all-gather.5
  299.7 44.7 all-gather.5
  371.3 44.7 all-gather.5
  443.1 44.4 all-gather.5
  514.6 44.4 all-gather.5
  586.3 43.5 all-gather.7
  657.1 43.5 all-gather.7
  727.9 43.5 all-gather.7
  798.7 43.5 all-gather.7
  869.5 43.5 all-gather.7
  940.2 43.5 all-gather.7
  1011.0 43.5 all-gather.7
  1093.9 652.2 reduce-scatter.1
where the time goes:
time: 1760 us; the launch traced here: 1750 us
  waiting for transfers between devices  1300 us (74%)
  local copies, waits for them, and re-layouts  202 us (11%)
  matrix products  154 us (9%)
  other arithmetic  66 us (4%)
  starting transfers between devices  18.8 us (1%)
    reduce_scatter x1, waiting for transfers between devices, shards(): lax.psum_scatter(local_sums, ('depth', 'plane'), scatter_dimension=1, til...  652 us
    all_gather x15, waiting for transfers between devices, apply_layer(): gathered = lax.all_gather(incoming, 'plane', axis=2, tiled=True)  626 us
    dot_general x15, matrix products, apply_layer(): jnp.einsum('rkiaj,vbrkj->vabri', factor, chosen, preferred_element_type=j...  154 us
    reshape x30, local copies, waits for them, and re-layouts, apply_layer(): blocks = gathered.reshape(rows_here, 2, -1, block_cells)  85.8 us
    gather x15, local copies, waits for them, and re-layouts, apply_layer(): chosen = jnp.take(blocks, pattern_flat, axis=2)  60.9 us
    select_n x30, other arithmetic, apply_layer(): chosen = jnp.take(blocks, pattern_flat, axis=2)  43 us
  transfers between devices with their start and end apart: 30, of which 30 were waited for; matrix products, arithmetic and copies ran while one was open for 3% of the time, Pallas kernels for 0%

commit v1 on v0

--- a/solution.py
+++ b/solution.py
@@ -29,7 +29,19 @@
     source = jnp.stack([real_part, imag_part], axis=1)
 
     def apply_layer(incoming):
-        gathered = lax.all_gather(incoming, "plane", axis=2, tiled=True)
+        shares = lax.axis_size("plane")
+        gallery = [(rr, (rr + 1) % shares) for rr in range(shares)]
+        far_arr, met_up = ([incoming], [incoming])
+        buffer = [(rr, (rr - 1) % shares) for rr in range(shares)]
+        for _ in range(shares // 2):
+            far_arr.append(lax.ppermute(far_arr[-1], "plane", gallery))
+        for _ in [*range((shares - 1) // 2)]:
+            upper = lax.ppermute(met_up[-1], "plane", perm=buffer)
+            met_up.append(upper)
+        side_arr = jnp.concatenate([*far_arr[::-1], *met_up[1:]], axis=2)
+        gathered = jnp.roll(
+            side_arr, (lax.axis_index("plane") - shares // 2) * incoming.shape[2], axis=2
+        )
         rows_here = gathered.shape[0]
         blocks = gathered.reshape(rows_here, 2, -1, block_cells)
         chosen = jnp.take(blocks, pattern_flat, axis=2)

time: 1760 us -> 2100 us (1.19)
  starting transfers between devices: 18.8 us -> 601 us
  waiting for transfers between devices: 1300 us -> 1040 us
  other arithmetic: 66 us -> 88.3 us
    all_gather x15 -> x0, waiting for transfers between devices: 626 us -> none  [apply_layer(): gathered = lax.all_gather(incoming, 'plane', axis=2, tiled=True)]
    ppermute x0 -> x225, starting transfers between devices: none -> 572 us  [the longest x105 570 us: apply_layer(): upper = lax.ppermute(met_up[-1], 'plane', perm=buffer)]
    ppermute x0 -> x225, waiting for transfers between devices: none -> 343 us  [the longest x120 339 us: apply_layer(): far_arr.append(lax.ppermute(far_arr[-1], 'plane', gallery))]
    concatenate x0 -> x15, other arithmetic: none -> 27.5 us  [apply_layer(): jnp.roll(side_arr, (lax.axis_index('plane') - shares // 2) * incoming.sha...]
  transfers between devices with their start and end apart: 30 -> 240, of which waited for: 30 -> 136; matrix products, arithmetic and copies ran while one was open for 3% -> 2% of each run, Pallas kernels for 0% -> 0%
where the time goes in v1:
time: 2100 us; the launch traced here: 2090 us
  waiting for transfers between devices  1040 us (50%)
  starting transfers between devices  601 us (29%)
  local copies, waits for them, and re-layouts  189 us (9%)
  matrix products  154 us (7%)
  other arithmetic  88.3 us (4%)
    reduce_scatter x1, waiting for transfers between devices, shards(): lax.psum_scatter(local_sums, ('depth', 'plane'), scatter_dimension=1, til...  665 us
    ppermute x105, starting transfers between devices, apply_layer(): upper = lax.ppermute(met_up[-1], 'plane', perm=buffer)  570 us
    ppermute x120, waiting for transfers between devices, apply_layer(): far_arr.append(lax.ppermute(far_arr[-1], 'plane', gallery))  339 us
    dot_general x15, matrix products, apply_layer(): jnp.einsum('rkiaj,vbrkj->vabri', factor, chosen, preferred_element_type=j...  154 us
    reshape x30, local copies, waits for them, and re-layouts, apply_layer(): blocks = gathered.reshape(rows_here, 2, -1, block_cells)  74.5 us
    gather x15, local copies, waits for them, and re-layouts, apply_layer(): chosen = jnp.take(blocks, pattern_flat, axis=2)  61.3 us
    select_n x30, other arithmetic, apply_layer(): chosen = jnp.take(blocks, pattern_flat, axis=2)  42.9 us
  transfers between devices with their start and end apart: 240, of which 136 were waited for; matrix products, arithmetic and copies ran while one was open for 2% of the time, Pallas kernels for 0%

profile of v1, /device:TPU:0, one launch (start us, length us, event | category | flops | bytes accessed | tf_op | source)
XLA Modules:
  0.0 2087.5 jit_solution(8631555505877537757)
XLA Ops:
  10.7 5.9 collective-permute-done.32
  47.5 5.8 collective-permute-start.44
  55.0 27.8 %reshape_squeeze.7 = bf16[32,16,64,2,64]{4,3,2,1,0:T(2,128)(2,1)} reshape(bf16[1,32,16,64,128]{4,3,2,1,0:T(8,128)(2,1)} %param.17) | data formatting | bytes 16777216 | tf_op jit(solution)/shard_map/reshape;squeeze | solution.py:25
  82.9 15.1 copy.28
  105.2 6.2 collective-permute-start.46
  125.7 13.0 fusion.26
  139.1 627.8 %while.24 = (s32[]{:T(128)}, bf16[8,2,2048]{2,0,1:T(8,128)(2,1)S(1)}, f32[1,2048]{1,0:T(1,128)S(1)}, f32[8,2,2048]{2,0,1:T(8,128)S(1)}, s32[512]{0:T(512)S(1)}, ...) while((s32[]{:T(128)}, ...), condition=%wide.region_1.4_spmd, body=%wide.region_0.3_spmd.sunk | while | flops 137074192 | bytes 27484112 | solution.py:64
  141.5 7.9 collective-permute-done.1
  217.3 10.1 fusion.50
  230.1 7.6 collective-permute-done.1
  268.0 5.6 collective-permute-start.13
  305.2 10.1 fusion.50
  317.9 7.6 collective-permute-done.1
  393.4 10.1 fusion.50
  407.6 7.6 collective-permute-done.1
  482.7 10.1 fusion.50
  498.1 7.6 collective-permute-done.1
  573.5 10.1 fusion.50
  589.9 7.6 collective-permute-done.1
  665.0 10.1 fusion.50
  680.9 7.6 collective-permute-done.1
  756.2 10.1 fusion.50
  766.9 630.4 %while.25 = (s32[]{:T(128)}, bf16[8,2,2048]{2,0,1:T(8,128)(2,1)S(1)}, bf16[8,2,2048]{2,0,1:T(8,128)(2,1)S(1)}, f32[1,2048]{1,0:T(1,128)S(1)}, s32[512]{0:T(512)S...) while((s32[]{:T(128)}, ...), condition=%wide.region_3.6_spmd, body=%wide.region_2.5_spmd.sunk | while | flops 137106960 | bytes 27811792 | solution.py:71
  772.6 7.6 collective-permute-done.17
  810.9 5.6 collective-permute-start.29
  826.1 5.6 collective-permute-start.31
  847.8 10.1 fusion.55
  864.0 7.6 collective-permute-done.17
  939.2 10.1 fusion.55
  954.0 7.6 collective-permute-done.17
  977.1 5.6 collective-permute-start.27
  984.7 5.6 collective-permute-start.28
  992.3 5.6 collective-permute-start.29
  999.9 5.6 collective-permute-start.30
  1007.5 5.6 collective-permute-start.31
  1029.2 10.1 fusion.55
  1043.1 7.6 collective-permute-done.17
  1118.2 10.1 fusion.55
  1132.2 7.6 collective-permute-done.17
  1155.0 5.7 collective-permute-start.27
  1207.3 10.1 fusion.55
  1222.0 7.6 collective-permute-done.17
  1297.1 10.1 fusion.55
  1311.6 7.6 collective-permute-done.17
  1334.3 5.7 collective-permute-start.27
  1386.6 10.1 fusion.55
  1397.7 15.4 scatter_custom_fusion
  1413.8 664.9 %reduce-scatter.2.cloned.1.call-done = f32[8,128]{0,1:T(8,128)} async-done(((f32[8,16384]{0,1:T(8,128)}), f32[8,128]{0,1:T(8,128)}) %reduce-scatter.2.cloned.1.call-update) | async-done | bytes 4112 | tf_op jit(solution)/shard_map/reduce_scatter | solution.py:78
  (934 shorter events, 1010.4 us)
Async XLA Ops:
  7.2 2071.5 %reduce-scatter.2.cloned.1.call-start = ((), (), s32[]{:S(2)}) async-start(), calls=%async_computation.1 | async-start | bytes 8454144 | tf_op jit(solution)/shard_map/reduce_scatter | solution.py:78
  31.8 8.5 collective-permute-start.42
  46.9 8.1 collective-permute-start.37
  47.5 50.5 %collective-permute-start.44 = (bf16[8,2,2048]{2,0,1:T(8,128)(2,1)S(1)}, bf16[8,2,2048]{2,0,1:T(8,128)(2,1)S(1)}, u32[]{:S(2)}, u32[]{:S(2)}) collective-permute-start(bf16[8,2,2048]{2,0,1:T(8,128)(2,1)S(1)} %collective-permute-done.43), channel_id=1, source_target_pairs={{0,15},{1,0},{2,1},{3,2},{4,3},{5,4},{6,5},{7,6},{8,7},{9,8},{10,9... | collective-permute-start | bytes 196616 | tf_op jit(solution)/shard_map/ppermute | solution.py:39
  55.0 48.3 %collective-permute-start.38 = (bf16[8,2,2048]{2,0,1:T(8,128)(2,1)S(1)}, bf16[8,2,2048]{2,0,1:T(8,128)(2,1)S(1)}, u32[]{:S(2)}, u32[]{:S(2)}) collective-permute-start(bf16[8,2,2048]{2,0,1:T(8,128)(2,1)S(1)} %collective-permute-done.37), channel_id=1, source_target_pairs={{0,1},{1,2},{2,3},{3,4},{4,5},{5,6},{6,7},{7,8},{8,9},{9,10},{10,1... | collective-permute-start | bytes 196616 | tf_op jit(solution)/shard_map/ppermute | solution.py:37
  103.3 8.1 collective-permute-start.39
  105.2 8.1 collective-permute-start.46
  141.5 8.0 collective-permute-start.1
  157.1 8.2 collective-permute-start.3
  157.1 8.2 collective-permute-start.10
  195.6 7.8 collective-permute-start.15
  268.0 7.9 collective-permute-start.6
  268.0 8.0 collective-permute-start.13
  283.5 7.8 collective-permute-start.15
  333.1 8.2 collective-permute-start.3
  333.1 8.2 collective-permute-start.10
  371.7 7.8 collective-permute-start.15
  430.3 7.9 collective-permute-start.4
  430.3 7.9 collective-permute-start.11
  461.0 7.8 collective-permute-start.15
  528.4 8.2 collective-permute-start.5
  528.4 8.2 collective-permute-start.12
  551.8 7.8 collective-permute-start.15
  643.3 7.8 collective-permute-start.15
  711.2 8.2 collective-permute-start.5
  711.2 8.2 collective-permute-start.12
  734.6 7.8 collective-permute-start.15
  802.9 8.0 collective-permute-start.21
  803.0 8.0 collective-permute-start.28
  826.1 7.8 collective-permute-start.31
  886.8 8.0 collective-permute-start.20
  886.8 8.0 collective-permute-start.27
  917.6 7.8 collective-permute-start.31
  969.1 8.0 collective-permute-start.19
  969.1 8.0 collective-permute-start.26
  1007.5 7.8 collective-permute-start.31
  1058.3 7.9 collective-permute-start.19
  1058.3 7.9 collective-permute-start.26
  1096.5 7.8 collective-permute-start.31
  1155.0 7.9 collective-permute-start.20
  1155.0 7.9 collective-permute-start.27
  1185.6 7.8 collective-permute-start.31
  1237.2 7.8 collective-permute-start.19
  1237.2 7.8 collective-permute-start.26
  1275.4 7.8 collective-permute-start.31
  1334.3 7.9 collective-permute-start.20
  1334.3 7.9 collective-permute-start.27
  1365.0 7.8 collective-permute-start.31
  (194 other events, 2051.7 us)
Sparse Core Ops, SparseCore 0:
  1413.2 665.4 reduce-scatter.1
